TPU v7x, 32 devices: a whole 2x2x4 slice. The times are simulated.
32 devices in a mesh: rep: 4 (over y, core), ep: 8 (over z, x).
Axes of the slice: x: 2, y: 2, z: 4, core: 2. Of those that a mesh axis runs over, the one named last changes fastest.
Arguments:
- tokens: bfloat16 [8192, 2048], P(('rep', 'ep')), may hold values from -6 to 6
- expert_ids: int32 [8192, 8], P(('rep', 'ep')), may hold values from 0 to 127, as said below
- gate_weights: float32 [8192, 8], P(('rep', 'ep')), may hold values from 0.25 to 1
- w_gate: bfloat16 [8, 768, 2048], P('ep'), may hold values from -0.125 to 0.125
- w_up: bfloat16 [8, 768, 2048], P('ep'), may hold values from -0.125 to 0.125
- w_down: bfloat16 [8, 768, 2048], P('ep'), may hold values from -0.21875 to 0.21875
- out_grad: bfloat16 [8192, 2048], P(('rep', 'ep')), may hold values from -6 to 6
Outputs:
- layer_out: bfloat16 [8192, 2048], P(('rep', 'ep'))
- tokens_grad: bfloat16 [8192, 2048], P(('rep', 'ep'))
- gates_grad: float32 [8192, 8], P(('rep', 'ep'))
- gate_w_grad: bfloat16 [8, 768, 2048], P('ep', 'rep')
- up_w_grad: bfloat16 [8, 768, 2048], P('ep', 'rep')
- down_w_grad: bfloat16 [8, 768, 2048], P('ep', 'rep')
Inputs may be any that keep to these rules, and one draw needn't show every extreme that they name: `expert_ids`: entry j of a row lies in [16 * j, 16 * j + 16); in the rows of one device no id below 8 appears more than 32 times, and some id below 8 appears exactly 32 times.
All inputs are finite; a program needn't handle non-finite values.
Results may differ from a plain program's by a relative error of at most 0.0065.
Values may be sent and summed in bfloat16 or wider, within the bound.
No kernel may reach another device: no remote copies, remote signals or barrier semaphores. Data moves between devices by JAX's collectives and lax.ppermute only.
A program may use at most 128 MiB of HBM per device.

v0:
```python
import jax
import jax.numpy as jnp
from jax import lax
from jax.sharding import PartitionSpec as P

STRIPE = 16


def silu_grad(value):
    sigmoid_value = jax.nn.sigmoid(value)
    return sigmoid_value * (1.0 + value * (1.0 - sigmoid_value))


def rows_times(left, right):
    return lax.dot_general(
        left, right, (((1,), (1,)), ((), ())), preferred_element_type=jnp.float32
    )


def inner_rows(left, right):
    return lax.dot_general(
        left, right, (((0,), (0,)), ((), ())), preferred_element_type=jnp.float32
    )


def matmul(left, right):
    return jnp.dot(left, right, preferred_element_type=jnp.float32)


def body(tokens, expert_ids, gate_weights, w_gate, w_up, w_down, out_grad):
    tok_count, feature_width = tokens.shape
    top_count = expert_ids.shape[1]
    experts = lax.axis_size("ep")
    per_pair = tok_count // 8
    total_slots = experts * per_pair
    live_cols = min(top_count, -(-experts // STRIPE))
    assigned = tok_count * live_cols
    flat_ids = expert_ids[:, :live_cols].reshape(-1)
    flat_gates = gate_weights[:, :live_cols].reshape(-1)
    live_mask = flat_ids < experts
    onehot = flat_ids[:, None] == jnp.arange(experts, dtype=jnp.int32)[None, :]
    position = jnp.arange(assigned, dtype=jnp.int32)
    earlier = (position[:, None] > position[None, :]).astype(jnp.bfloat16)
    before = matmul(earlier, onehot.astype(jnp.bfloat16))
    slot_rank = jnp.sum(jnp.where(onehot, before, 0.0), axis=1).astype(jnp.int32)
    slot_index = jnp.where(live_mask, flat_ids * per_pair + slot_rank, -1)
    slot_ids = jnp.arange(total_slots, dtype=jnp.int32)
    hit = slot_ids[:, None] == slot_index[None, :]
    slot_gate = jnp.sum(jnp.where(hit, flat_gates[None, :], 0.0), axis=1)
    pick = jnp.any(hit.reshape(total_slots, tok_count, live_cols), axis=2).astype(jnp.bfloat16)
    send_rows = matmul(pick, tokens).astype(jnp.bfloat16)
    grad_rows = matmul(pick, out_grad)
    scaled_grad = (slot_gate[:, None] * grad_rows).astype(jnp.bfloat16)

    def exchange(rows):
        return lax.all_to_all(
            rows.reshape(experts, per_pair, feature_width),
            "ep",
            split_axis=0,
            concat_axis=0,
            tiled=True,
        ).reshape(total_slots, feature_width)

    rows_in = exchange(send_rows)
    grad_in = exchange(scaled_grad)
    copies = lax.axis_size("rep")
    by_pieces = copies == 4

    def to_copy(values, step):
        return lax.ppermute(values, "rep", [(r, r ^ step) for r in range(copies)])

    if by_pieces:
        far_rows = to_copy(rows_in, 2)
        near_rows = to_copy(rows_in, 1)
    else:
        gathered_rows = lax.all_gather(rows_in, "rep", axis=0, tiled=True)
        gathered_grad = lax.all_gather(grad_in, "rep", axis=0, tiled=True)
    gate_mat = w_gate[0]
    up_mat = w_up[0]
    down_mat = w_down[0]
    gate_up_mat = jnp.concatenate([gate_mat, up_mat], axis=0)
    hidden_units = gate_mat.shape[0]
    pre_both_own = rows_times(rows_in, gate_up_mat)
    pre_gate = pre_both_own[:, :hidden_units]
    pre_up = pre_both_own[:, hidden_units:]
    activated = jax.nn.silu(pre_gate)
    hidden = (activated * pre_up).astype(jnp.bfloat16)
    expert_out = matmul(hidden, down_mat).astype(jnp.bfloat16)
    expert_out, grad_in = lax.optimization_barrier((expert_out, grad_in))
    returned = lax.all_to_all(
        expert_out.reshape(experts, per_pair, feature_width),
        "ep",
        split_axis=0,
        concat_axis=0,
        tiled=True,
    ).reshape(total_slots, feature_width)
    hidden_grad = rows_times(grad_in, down_mat)
    gate_pre_grad = (hidden_grad * pre_up * silu_grad(pre_gate)).astype(jnp.bfloat16)
    up_pre_grad = (hidden_grad * activated).astype(jnp.bfloat16)
    token_part = matmul(jnp.concatenate([gate_pre_grad, up_pre_grad], axis=1), gate_up_mat).astype(
        jnp.bfloat16
    )
    if by_pieces:
        token_part, grad_out = lax.optimization_barrier((token_part, grad_in))
        far_grad = to_copy(grad_out, 2)
        near_grad = to_copy(grad_out, 1)
    part_back = lax.all_to_all(
        token_part.reshape(experts, per_pair, feature_width),
        "ep",
        split_axis=0,
        concat_axis=0,
        tiled=True,
    ).reshape(total_slots, feature_width)
    if by_pieces:
        returned, near_rows, near_grad = lax.optimization_barrier((returned, near_rows, near_grad))
    slot_grid = slot_index.reshape(tok_count, live_cols)
    gate_grid = flat_gates.reshape(tok_count, live_cols)
    layer_sum = jnp.zeros((tok_count, feature_width), jnp.float32)
    gate_cols = []
    back_pick = jnp.zeros((tok_count, total_slots), jnp.bfloat16)
    for col in range(live_cols):
        col_pick = (slot_grid[:, col : col + 1] == slot_ids[None, :]).astype(jnp.bfloat16)
        back_pick = back_pick + col_pick
        out_rows = matmul(col_pick, returned)
        layer_sum = layer_sum + gate_grid[:, col : col + 1] * out_rows
        gate_cols.append(jnp.sum(out_grad.astype(jnp.float32) * out_rows, axis=1))
    if by_pieces:
        layer_sum, far_rows, far_grad = lax.optimization_barrier((layer_sum, far_rows, far_grad))
        pieces = [
            (rows_in, grad_in),
            (near_rows, near_grad),
            (far_rows, far_grad),
            (to_copy(far_rows, 1), to_copy(far_grad, 1)),
        ]
    else:
        pieces = [(gathered_rows, gathered_grad)]
    layer_out = layer_sum.astype(jnp.bfloat16)
    gate_cols.extend([jnp.zeros((tok_count,), jnp.float32)] * (top_count - live_cols))
    gates_grad = jnp.stack(gate_cols, axis=1)
    share = gate_mat.shape[0] // copies
    start = lax.axis_index("rep") * share
    gate_share = lax.dynamic_slice_in_dim(gate_mat, start, share, axis=0)
    up_share = lax.dynamic_slice_in_dim(up_mat, start, share, axis=0)
    down_share = lax.dynamic_slice_in_dim(down_mat, start, share, axis=0)
    both_sum = None
    down_sum = None
    stacked_share = jnp.concatenate([gate_share, up_share], axis=0)
    for rows_p, grad_p in pieces:
        pre_both = rows_times(rows_p, stacked_share)
        pre_gate_s = pre_both[:, :share]
        pre_up_s = pre_both[:, share:]
        activated_s = jax.nn.silu(pre_gate_s)
        hidden_s = (activated_s * pre_up_s).astype(jnp.bfloat16)
        hidden_grad_s = rows_times(grad_p, down_share)
        gate_pre_grad_s = (hidden_grad_s * pre_up_s * silu_grad(pre_gate_s)).astype(jnp.bfloat16)
        up_pre_grad_s = (hidden_grad_s * activated_s).astype(jnp.bfloat16)
        both_p = inner_rows(jnp.concatenate([gate_pre_grad_s, up_pre_grad_s], axis=1), rows_p)
        down_p = inner_rows(hidden_s, grad_p)
        both_sum = both_p if both_sum is None else both_sum + both_p
        down_sum = down_p if down_sum is None else down_sum + down_p
    gate_w_grad = both_sum[:share].astype(jnp.bfloat16)[None]
    up_w_grad = both_sum[share:].astype(jnp.bfloat16)[None]
    down_w_grad = down_sum.astype(jnp.bfloat16)[None]
    part_back, gate_w_grad, up_w_grad, down_w_grad = lax.optimization_barrier(
        (part_back, gate_w_grad, up_w_grad, down_w_grad)
    )
    tokens_grad = matmul(back_pick, part_back).astype(jnp.bfloat16)
    return (layer_out, tokens_grad, gates_grad, gate_w_grad, up_w_grad, down_w_grad)


def solution(mesh):
    return jax.shard_map(
        body,
        mesh=mesh,
        in_specs=(
            P(("rep", "ep"), None),
            P(("rep", "ep"), None),
            P(("rep", "ep"), None),
            P("ep", None, None),
            P("ep", None, None),
            P("ep", None, None),
            P(("rep", "ep"), None),
        ),
        out_specs=(
            P(("rep", "ep"), None),
            P(("rep", "ep"), None),
            P(("rep", "ep"), None),
            P("ep", "rep", None),
            P("ep", "rep", None),
            P("ep", "rep", None),
        ),
        check_vma=False,
    )
```

profile of v0, /device:TPU:0, one launch (start us, length us, event | category | flops | bytes accessed | tf_op | source)
XLA Modules:
  0.0 129.3 jit_solution(9352168649783690748)
XLA Ops:
  1.7 2.6 %convolution_convert_fusion.1 = bf16[256,2048]{1,0:T(8,128)(2,1)} fusion(bf16[256,2048]{1,0:T(8,128)(2,1)} %param.7, s32[256]{0:T(256)S(1)} %compare_select_fusion.1), kind=kOutput, calls=%fused_computation.14 | convolution fusion | flops 269025280 | bytes 2098176 | tf_op jit(solution)/shard_map/dot_general | solution.py:27
  4.4 7.3 %all-to-all-start = ((bf16[8,32,2048]{2,1,0:T(8,128)(2,1)}), bf16[8,32,2048]{2,1,0:T(8,128)(2,1)}, u32[]{:S(2)}, u32[]{:S(2)}) async-start(bf16[8,32,2048]{2,1,0:T(8,128)(2,1)} %bitcast.75), calls=%async_computation | async-start | bytes 2097152 | tf_op jit(solution)/shard_map/all_to_all | solution.py:56
  12.4 2.6 %fusion.6 = bf16[256,2048]{1,0:T(8,128)(2,1)} fusion(bf16[256,2048]{1,0:T(8,128)(2,1)} %param.13, f32[256]{0:T(256)S(1)} %select_reduce_fusion, s32[256]{0:T(256)S(1)} %compare_select_fusion.1), kind=kOutput, calls=%fused_computation.11 | convolution fusion | flops 269549568 | bytes 2099200 | tf_op jit(solution)/shard_map/dot_general | solution.py:27
  15.1 22.4 %all-to-all-done = bf16[8,32,2048]{2,1,0:T(8,128)(2,1)} async-done(((bf16[8,32,2048]{2,1,0:T(8,128)(2,1)}), bf16[8,32,2048]{2,1,0:T(8,128)(2,1)}, u32[]{:S(2)}, u32[]{:S(2)}) %all-to-all-start) | async-done | bytes 1048608 | tf_op jit(solution)/shard_map/all_to_all | solution.py:56
  37.5 4.3 %all-to-all-start.1 = ((bf16[8,32,2048]{2,1,0:T(8,128)(2,1)}), bf16[8,32,2048]{2,1,0:T(8,128)(2,1)}, u32[]{:S(2)}, u32[]{:S(2)}) async-start(bf16[8,32,2048]{2,1,0:T(8,128)(2,1)} %bitcast.74), calls=%async_computation.1 | async-start | bytes 2097152 | tf_op jit(solution)/shard_map/all_to_all | solution.py:56
  42.9 2.8 %dynamic-slice_bitcast_fusion = (bf16[192,2048]{1,0:T(8,128)(2,1)}, bf16[192,2048]{1,0:T(8,128)(2,1)}) fusion(bf16[1,768,2048]{2,1,0:T(8,128)(2,1)} %param.11, s32[]{:T(128)S(6)} %select_n.28, bf16[1,768,2048]{2,1,0:T(8,128)(2,1)} %param.10), kind=kLoop, calls=%fused_computation.37 | loop fusion | bytes 3145732 | tf_op jit(solution)/shard_map/dynamic_slice | solution.py:143
  45.7 1.5 %collective-permute-start.2 = (bf16[256,2048]{1,0:T(8,128)(2,1)}, bf16[256,2048]{1,0:T(8,128)(2,1)}, u32[]{:S(2)}, u32[]{:S(2)}) collective-permute-start(bf16[256,2048]{1,0:T(8,128)(2,1)} %bitcast.5), channel_id=1, source_target_pairs={{0,16},{8,24},{16,0},{24,8},{1,17},{9,25},{17,1},{25,9},{2,18},{10... | collective-permute-start | bytes 3145736 | tf_op jit(solution)/shard_map/ppermute | solution.py:70
  47.2 4.0 %fusion.1 = f32[256,1536]{1,0:T(8,128)S(1)} fusion(bf16[256,2048]{1,0:T(8,128)(2,1)} %bitcast.5, bf16[768,2048]{1,0:T(8,128)(2,1)S(1)} %bitcast.78, bf16[768,2048]{1,0:T(8,128)(2,1)} %bitcast.80), kind=kOutput, calls=%fused_computation.2 | convolution fusion | flops 1623195648 | bytes 8912896 | tf_op jit(solution)/shard_map/dot_general | solution.py:15
  52.4 2.0 %fusion.9 = bf16[256,2048]{1,0:T(8,128)(2,1)} fusion(bf16[1,768,2048]{2,1,0:T(8,128)(2,1)S(1)} %copy-done, f32[256,1536]{1,0:T(8,128)S(1)} %fusion.1), kind=kOutput, calls=%fused_computation.16 | convolution fusion | flops 807010304 | bytes 5767168 | tf_op jit(solution)/shard_map/dot_general | solution.py:27
  54.4 12.9 %all-to-all-done.1 = bf16[8,32,2048]{2,1,0:T(8,128)(2,1)} async-done(((bf16[8,32,2048]{2,1,0:T(8,128)(2,1)}), bf16[8,32,2048]{2,1,0:T(8,128)(2,1)}, u32[]{:S(2)}, u32[]{:S(2)}) %all-to-all-start.1) | async-done | bytes 1048608 | tf_op jit(solution)/shard_map/all_to_all | solution.py:56
  67.3 4.2 %all-to-all-start.2 = ((bf16[8,32,2048]{2,1,0:T(8,128)(2,1)}), bf16[8,32,2048]{2,1,0:T(8,128)(2,1)}, u32[]{:S(2)}, u32[]{:S(2)}) async-start(bf16[8,32,2048]{2,1,0:T(8,128)(2,1)} %bitcast.77), calls=%async_computation.2 | async-start | bytes 2097152 | tf_op jit(solution)/shard_map/all_to_all | solution.py:90
  71.6 3.0 %multiply_convert_fusion.1 = (bf16[256,768]{1,0:T(8,128)(2,1)S(1)}, bf16[256,768]{1,0:T(8,128)(2,1)S(1)}) fusion(f32[256,1536]{1,0:T(8,128)} %copy-done.11, bf16[256,2048]{1,0:T(8,128)(2,1)} %bitcast.10, bf16[1,768,2048]{2,1,0:T(8,128)(2,1)S(1)} %copy-done), kind=kOutput, calls=%fused_computation.40 | convolution fusion | flops 807862272 | bytes 6553600 | tf_op jit(solution)/shard_map/dot_general | solution.py:15
  75.2 2.8 %fusion.7 = bf16[256,2048]{1,0:T(8,128)(2,1)} fusion(bf16[768,2048]{1,0:T(8,128)(2,1)S(1)} %bitcast.79, bf16[768,2048]{1,0:T(8,128)(2,1)S(1)} %bitcast.81, bf16[256,768]{1,0:T(8,128)(2,1)S(1)} %get-tuple-element.35, bf16[256,768]{1,0:T(8,128)(2,1)S(1)} %get-tuple-element.34), kind=kOutput, calls=%fused_computation.12 | convolution fusion | flops 1625292800 | bytes 8126464 | tf_op jit(solution)/shard_map/dot_general | solution.py:27
  78.1 1.5 %collective-permute-start.3 = (bf16[256,2048]{1,0:T(8,128)(2,1)}, bf16[256,2048]{1,0:T(8,128)(2,1)}, u32[]{:S(2)}, u32[]{:S(2)}) collective-permute-start(bf16[256,2048]{1,0:T(8,128)(2,1)} %bitcast.10), channel_id=1, source_target_pairs={{0,16},{8,24},{16,0},{24,8},{1,17},{9,25},{17,1},{25,9},{2,18},{10... | collective-permute-start | bytes 3145736 | tf_op jit(solution)/shard_map/ppermute | solution.py:70
  79.6 1.8 %fusion.84 = f32[256,384]{0,1:T(8,128)S(1)} fusion(bf16[256,2048]{1,0:T(8,128)(2,1)} %bitcast.5, bf16[192,2048]{1,0:T(8,128)(2,1)S(1)} %copy-done.4, bf16[192,2048]{1,0:T(8,128)(2,1)S(1)} %copy-done.6), kind=kOutput, calls=%fused_computation.118 | convolution fusion | flops 405798912 | bytes 3014656 | tf_op jit(solution)/shard_map/dot_general | solution.py:15
  81.4 1.7 %multiply_convert_fusion.15 = (bf16[256,192]{0,1:T(8,128)(2,1)S(1)}, bf16[256,192]{0,1:T(8,128)(2,1)S(1)}) fusion(f32[256,384]{0,1:T(8,128)S(1)} %fusion.84, bf16[256,2048]{1,0:T(8,128)(2,1)} %bitcast.10, bf16[1,768,2048]{2,1,0:T(8,128)(2,1)S(1)} %copy-done, s32[]{:T(128)S(6)} %select_n.28), kind=kOutput, calls=%fused_computation.86 | convolution fusion | flops 201965568 | bytes 2424836 | tf_op jit(solution)/shard_map/dot_general | solution.py:15
  83.2 2.8 %fusion.58 = f32[192,2048]{1,0:T(8,128)} fusion(bf16[256,2048]{1,0:T(8,128)(2,1)} %bitcast.10, f32[256,384]{0,1:T(8,128)S(1)} %fusion.84), kind=kOutput, calls=%fused_computation.93 | convolution fusion | flops 201621504 | bytes 3014656 | tf_op jit(solution)/shard_map/dot_general | solution.py:21
  85.9 3.4 %fusion.32 = f32[384,2048]{1,0:T(8,128)} fusion(bf16[256,2048]{1,0:T(8,128)(2,1)} %bitcast.5, bf16[256,192]{0,1:T(8,128)(2,1)S(1)} %get-tuple-element.43, bf16[256,192]{0,1:T(8,128)(2,1)S(1)} %get-tuple-element.42), kind=kOutput, calls=%fused_computation.53 | convolution fusion | flops 403046400 | bytes 4390912 | tf_op jit(solution)/shard_map/dot_general | solution.py:21
  89.4 7.6 %all-to-all-done.2 = bf16[8,32,2048]{2,1,0:T(8,128)(2,1)} async-done(((bf16[8,32,2048]{2,1,0:T(8,128)(2,1)}), bf16[8,32,2048]{2,1,0:T(8,128)(2,1)}, u32[]{:S(2)}, u32[]{:S(2)}) %all-to-all-start.2) | async-done | bytes 1048608 | tf_op jit(solution)/shard_map/all_to_all | solution.py:90
  97.0 4.4 %all-to-all-start.3 = ((bf16[8,32,2048]{2,1,0:T(8,128)(2,1)}), bf16[8,32,2048]{2,1,0:T(8,128)(2,1)}, u32[]{:S(2)}, u32[]{:S(2)}) async-start(bf16[8,32,2048]{2,1,0:T(8,128)(2,1)} %bitcast.76), calls=%async_computation.3 | async-start | bytes 2097152 | tf_op jit(solution)/shard_map/all_to_all | solution.py:107
  101.5 2.8 %broadcast_multiply_fusion = (bf16[256,2048]{1,0:T(8,128)(2,1)}, f32[256,2048]{1,0:T(8,128)S(1)}) fusion(f32[256]{0:T(256)S(1)} %bitcast.85, bf16[256,2048]{1,0:T(8,128)(2,1)} %bitcast.12, s32[256]{0:T(256)S(1)} %bitcast.82), kind=kOutput, calls=%fused_computation.23 | convolution fusion | flops 269549568 | bytes 4196352 | tf_op jit(solution)/shard_map/dot_general | solution.py:27
  104.3 1.8 %fusion.82 = f32[256,384]{0,1:T(8,128)S(1)} fusion(bf16[256,2048]{1,0:T(8,128)(2,1)} %collective-permute-done.2, bf16[192,2048]{1,0:T(8,128)(2,1)S(1)} %copy-done.5, bf16[192,2048]{1,0:T(8,128)(2,1)S(1)} %copy-done.7), kind=kOutput, calls=%fused_computation.116 | convolution fusion | flops 405798912 | bytes 3014656 | tf_op jit(solution)/shard_map/dot_general | solution.py:15
  106.2 1.8 %fusion.83 = f32[256,384]{0,1:T(8,128)S(1)} fusion(bf16[256,2048]{1,0:T(8,128)(2,1)} %collective-permute-done, bf16[192,2048]{1,0:T(8,128)(2,1)S(1)} %copy-done.5, bf16[192,2048]{1,0:T(8,128)(2,1)S(1)} %copy-done.7), kind=kOutput, calls=%fused_computation.117 | convolution fusion | flops 405798912 | bytes 3014656 | tf_op jit(solution)/shard_map/dot_general | solution.py:15
  108.6 1.7 %multiply_convert_fusion.11 = (bf16[256,192]{0,1:T(8,128)(2,1)S(1)}, bf16[256,192]{0,1:T(8,128)(2,1)S(1)}) fusion(f32[256,384]{0,1:T(8,128)S(1)} %fusion.82, bf16[256,2048]{1,0:T(8,128)(2,1)} %collective-permute-done.3, bf16[1,768,2048]{2,1,0:T(8,128)(2,1)S(1)} %copy-done, s32[]{:T(128)S(6)} %select_n.28), kind=kOutput, calls=%fused_computation.78 | convolution fusion | flops 201965568 | bytes 2424836 | tf_op jit(solution)/shard_map/dot_general | solution.py:15
  110.3 1.8 %multiply_convert_fusion.13 = (bf16[256,192]{0,1:T(8,128)(2,1)S(1)}, bf16[256,192]{0,1:T(8,128)(2,1)S(1)}) fusion(f32[256,384]{0,1:T(8,128)S(1)} %fusion.83, bf16[256,2048]{1,0:T(8,128)(2,1)} %collective-permute-done.1, bf16[1,768,2048]{2,1,0:T(8,128)(2,1)S(1)} %copy-done, s32[]{:T(128)S(6)} %select_n.28), kind=kOutput, calls=%fused_computation.82 | convolution fusion | flops 201965568 | bytes 2424836 | tf_op jit(solution)/shard_map/dot_general | solution.py:15
  112.2 1.8 %fusion.36 = f32[384,2048]{1,0:T(8,128)S(1)} fusion(bf16[256,2048]{1,0:T(8,128)(2,1)} %collective-permute-done, bf16[256,192]{0,1:T(8,128)(2,1)S(1)} %get-tuple-element.41, bf16[256,192]{0,1:T(8,128)(2,1)S(1)} %get-tuple-element.40), kind=kOutput, calls=%fused_computation.57 | convolution fusion | flops 403046400 | bytes 4390912 | tf_op jit(solution)/shard_map/dot_general | solution.py:21
  115.0 1.8 %fusion.40 = f32[384,2048]{1,0:T(8,128)S(1)} fusion(bf16[256,2048]{1,0:T(8,128)(2,1)} %collective-permute-done.2, bf16[256,192]{0,1:T(8,128)(2,1)S(1)} %get-tuple-element.45, bf16[256,192]{0,1:T(8,128)(2,1)S(1)} %get-tuple-element.44), kind=kOutput, calls=%fused_computation.61 | convolution fusion | flops 403046400 | bytes 4390912 | tf_op jit(solution)/shard_map/dot_general | solution.py:21
  116.8 1.6 %convolution_add_fusion.1 = f32[192,2048]{1,0:T(8,128)S(1)} fusion(f32[192,2048]{1,0:T(8,128)S(1)} %copy-done.2, bf16[256,2048]{1,0:T(8,128)(2,1)} %collective-permute-done.1, f32[256,384]{0,1:T(8,128)S(1)} %fusion.83), kind=kOutput, calls=%fused_computation.10 | convolution fusion | flops 202014720 | bytes 4587520 | tf_op jit(solution)/shard_map/dot_general | solution.py:21
  120.0 2.7 %fusion.13 = bf16[1,192,2048]{2,1,0:T(8,128)(2,1)} fusion(f32[192,2048]{1,0:T(8,128)S(1)} %fusion.59, f32[192,2048]{1,0:T(8,128)S(1)} %convolution_add_fusion.1, bf16[256,2048]{1,0:T(8,128)(2,1)} %collective-permute-done.3, f32[256,384]{0,1:T(8,128)S(1)} %fusion.82), kind=kOutput, calls=%fused_computation.18 | convolution fusion | flops 202801152 | bytes 5373952 | tf_op jit(solution)/shard_map/dot_general | solution.py:21
  123.3 1.2 slice_bitcast_fusion
  124.5 2.1 %all-to-all-done.3 = bf16[8,32,2048]{2,1,0:T(8,128)(2,1)} async-done(((bf16[8,32,2048]{2,1,0:T(8,128)(2,1)}), bf16[8,32,2048]{2,1,0:T(8,128)(2,1)}, u32[]{:S(2)}, u32[]{:S(2)}) %all-to-all-start.3) | async-done | bytes 1048608 | tf_op jit(solution)/shard_map/all_to_all | solution.py:107
  126.6 2.7 %convolution_convert_fusion = bf16[256,2048]{1,0:T(8,128)(2,1)} fusion(bf16[256,2048]{1,0:T(8,128)(2,1)} %bitcast.14, s32[256]{0:T(256)S(1)} %bitcast.83), kind=kOutput, calls=%fused_computation.13 | convolution fusion | flops 269025280 | bytes 2098176 | tf_op jit(solution)/shard_map/dot_general | solution.py:27
  (52 shorter events, 8.5 us)
Async XLA Ops:
  0.6 51.8 %copy-start = (bf16[1,768,2048]{2,1,0:T(8,128)(2,1)S(1)}, bf16[1,768,2048]{2,1,0:T(8,128)(2,1)}, u32[]{:S(2)}) copy-start(bf16[1,768,2048]{2,1,0:T(8,128)(2,1)} %param.12) | copy-start | bytes 9437188
  4.4 33.1 %all-to-all-start = ((bf16[8,32,2048]{2,1,0:T(8,128)(2,1)}), bf16[8,32,2048]{2,1,0:T(8,128)(2,1)}, u32[]{:S(2)}, u32[]{:S(2)}) async-start(bf16[8,32,2048]{2,1,0:T(8,128)(2,1)} %bitcast.75), calls=%async_computation | async-start | bytes 2097152 | tf_op jit(solution)/shard_map/all_to_all | solution.py:56
  37.5 29.9 %all-to-all-start.1 = ((bf16[8,32,2048]{2,1,0:T(8,128)(2,1)}), bf16[8,32,2048]{2,1,0:T(8,128)(2,1)}, u32[]{:S(2)}, u32[]{:S(2)}) async-start(bf16[8,32,2048]{2,1,0:T(8,128)(2,1)} %bitcast.74), calls=%async_computation.1 | async-start | bytes 2097152 | tf_op jit(solution)/shard_map/all_to_all | solution.py:56
  42.0 5.2 %copy-start.8 = (bf16[1,768,2048]{2,1,0:T(8,128)(2,1)S(1)}, bf16[1,768,2048]{2,1,0:T(8,128)(2,1)}, u32[]{:S(2)}) copy-start(bf16[1,768,2048]{2,1,0:T(8,128)(2,1)} %param.11) | copy-start | bytes 9437188
  45.7 58.6 %collective-permute-start.2 = (bf16[256,2048]{1,0:T(8,128)(2,1)}, bf16[256,2048]{1,0:T(8,128)(2,1)}, u32[]{:S(2)}, u32[]{:S(2)}) collective-permute-start(bf16[256,2048]{1,0:T(8,128)(2,1)} %bitcast.5), channel_id=1, source_target_pairs={{0,16},{8,24},{16,0},{24,8},{1,17},{9,25},{17,1},{25,9},{2,18},{10... | collective-permute-start | bytes 3145736 | tf_op jit(solution)/shard_map/ppermute | solution.py:70
  47.2 54.3 %collective-permute-start = (bf16[256,2048]{1,0:T(8,128)(2,1)}, bf16[256,2048]{1,0:T(8,128)(2,1)}, u32[]{:S(2)}, u32[]{:S(2)}) collective-permute-start(bf16[256,2048]{1,0:T(8,128)(2,1)} %bitcast.5), channel_id=1, source_target_pairs={{0,8},{8,0},{16,24},{24,16},{1,9},{9,1},{17,25},{25,17},{2,10},{10... | collective-permute-start | bytes 3145736 | tf_op jit(solution)/shard_map/ppermute | solution.py:70
  51.2 1.2 copy-start.11
  67.3 29.6 %all-to-all-start.2 = ((bf16[8,32,2048]{2,1,0:T(8,128)(2,1)}), bf16[8,32,2048]{2,1,0:T(8,128)(2,1)}, u32[]{:S(2)}, u32[]{:S(2)}) async-start(bf16[8,32,2048]{2,1,0:T(8,128)(2,1)} %bitcast.77), calls=%async_computation.2 | async-start | bytes 2097152 | tf_op jit(solution)/shard_map/all_to_all | solution.py:90
  71.6 3.1 %copy-start.9 = (bf16[1,768,2048]{2,1,0:T(8,128)(2,1)S(1)}, bf16[1,768,2048]{2,1,0:T(8,128)(2,1)}, u32[]{:S(2)}) copy-start(bf16[1,768,2048]{2,1,0:T(8,128)(2,1)} %param.11) | copy-start | bytes 9437188
  71.6 3.6 %copy-start.10 = (bf16[1,768,2048]{2,1,0:T(8,128)(2,1)S(1)}, bf16[1,768,2048]{2,1,0:T(8,128)(2,1)}, u32[]{:S(2)}) copy-start(bf16[1,768,2048]{2,1,0:T(8,128)(2,1)} %param.10) | copy-start | bytes 9437188
  75.2 4.3 %copy-start.4 = (bf16[192,2048]{1,0:T(8,128)(2,1)S(1)}, bf16[192,2048]{1,0:T(8,128)(2,1)}, u32[]{:S(2)}) copy-start(bf16[192,2048]{1,0:T(8,128)(2,1)} %get-tuple-element.48) | copy-start | bytes 2359300
  75.2 4.3 %copy-start.6 = (bf16[192,2048]{1,0:T(8,128)(2,1)S(1)}, bf16[192,2048]{1,0:T(8,128)(2,1)}, u32[]{:S(2)}) copy-start(bf16[192,2048]{1,0:T(8,128)(2,1)} %get-tuple-element.49) | copy-start | bytes 2359300
  78.1 26.2 %collective-permute-start.3 = (bf16[256,2048]{1,0:T(8,128)(2,1)}, bf16[256,2048]{1,0:T(8,128)(2,1)}, u32[]{:S(2)}, u32[]{:S(2)}) collective-permute-start(bf16[256,2048]{1,0:T(8,128)(2,1)} %bitcast.10), channel_id=1, source_target_pairs={{0,16},{8,24},{16,0},{24,8},{1,17},{9,25},{17,1},{25,9},{2,18},{10... | collective-permute-start | bytes 3145736 | tf_op jit(solution)/shard_map/ppermute | solution.py:70
  79.6 21.9 %collective-permute-start.1 = (bf16[256,2048]{1,0:T(8,128)(2,1)}, bf16[256,2048]{1,0:T(8,128)(2,1)}, u32[]{:S(2)}, u32[]{:S(2)}) collective-permute-start(bf16[256,2048]{1,0:T(8,128)(2,1)} %bitcast.10), channel_id=1, source_target_pairs={{0,8},{8,0},{16,24},{24,16},{1,9},{9,1},{17,25},{25,17},{2,10},{10... | collective-permute-start | bytes 3145736 | tf_op jit(solution)/shard_map/ppermute | solution.py:70
  97.0 29.6 %all-to-all-start.3 = ((bf16[8,32,2048]{2,1,0:T(8,128)(2,1)}), bf16[8,32,2048]{2,1,0:T(8,128)(2,1)}, u32[]{:S(2)}, u32[]{:S(2)}) async-start(bf16[8,32,2048]{2,1,0:T(8,128)(2,1)} %bitcast.76), calls=%async_computation.3 | async-start | bytes 2097152 | tf_op jit(solution)/shard_map/all_to_all | solution.py:107
  101.4 2.9 %copy-start.5 = (bf16[192,2048]{1,0:T(8,128)(2,1)S(1)}, bf16[192,2048]{1,0:T(8,128)(2,1)}, u32[]{:S(2)}) copy-start(bf16[192,2048]{1,0:T(8,128)(2,1)} %get-tuple-element.48) | copy-start | bytes 2359300
  101.4 2.8 %copy-start.7 = (bf16[192,2048]{1,0:T(8,128)(2,1)S(1)}, bf16[192,2048]{1,0:T(8,128)(2,1)}, u32[]{:S(2)}) copy-start(bf16[192,2048]{1,0:T(8,128)(2,1)} %get-tuple-element.49) | copy-start | bytes 2359300
  106.1 12.3 %collective-permute-start.5 = (bf16[256,2048]{1,0:T(8,128)(2,1)}, bf16[256,2048]{1,0:T(8,128)(2,1)S(1)}, u32[]{:S(2)}, u32[]{:S(2)}) collective-permute-start(bf16[256,2048]{1,0:T(8,128)(2,1)} %collective-permute-done.2), channel_id=1, source_target_pairs={{0,8},{8,0},{16,24},{24,16},{1,9},{9,1},{17,25},{25,17},{2,10},{10... | collective-permute-start | bytes 3145736 | tf_op jit(solution)/shard_map/ppermute | solution.py:70
  108.0 11.0 %collective-permute-start.4 = (bf16[256,2048]{1,0:T(8,128)(2,1)}, bf16[256,2048]{1,0:T(8,128)(2,1)S(1)}, u32[]{:S(2)}, u32[]{:S(2)}) collective-permute-start(bf16[256,2048]{1,0:T(8,128)(2,1)} %collective-permute-done.3), channel_id=1, source_target_pairs={{0,8},{8,0},{16,24},{24,16},{1,9},{9,1},{17,25},{25,17},{2,10},{10... | collective-permute-start | bytes 3145736 | tf_op jit(solution)/shard_map/ppermute | solution.py:70
  110.3 3.7 %copy-start.3 = (bf16[256,2048]{1,0:T(8,128)(2,1)S(1)}, bf16[256,2048]{1,0:T(8,128)(2,1)}, u32[]{:S(2)}) copy-start(bf16[256,2048]{1,0:T(8,128)(2,1)} %param.13) | copy-start | bytes 3145732
  114.0 2.8 %copy-start.2 = (f32[192,2048]{1,0:T(8,128)S(1)}, f32[192,2048]{1,0:T(8,128)}, u32[]{:S(2)}) copy-start(f32[192,2048]{1,0:T(8,128)} %fusion.58) | copy-start | bytes 4718596
  120.0 2.7 %copy-start.1 = (f32[384,2048]{1,0:T(8,128)S(1)}, f32[384,2048]{1,0:T(8,128)}, u32[]{:S(2)}) copy-start(f32[384,2048]{1,0:T(8,128)} %fusion.32) | copy-start | bytes 9437188
where the time goes:
time: 130 us; the launch traced here: 129 us
  matrix products  49.9 us (38%)
  waiting for transfers between devices  45.1 us (35%)
  starting transfers between devices  23.8 us (18%)
  local copies, waits for them, and re-layouts  7.6 us (6%)
  other arithmetic  1.94 us (1%)
    all_to_all x2, waiting for transfers between devices, exchange(): lax.all_to_all(rows.reshape(experts, per_pair, feature_width), 'ep', spli...  35.4 us
    dot_general x10, matrix products, rows_times(): lax.dot_general(left, right, (((1,), (1,)), ((), ())), preferred_element_...  19 us
    dot_general x7, matrix products, matmul(): return jnp.dot(left, right, preferred_element_type=jnp.float32)  15.8 us
    dot_general x8, matrix products, inner_rows(): lax.dot_general(left, right, (((0,), (0,)), ((), ())), preferred_element_...  15.1 us
    all_to_all x2, starting transfers between devices, exchange(): lax.all_to_all(rows.reshape(experts, per_pair, feature_width), 'ep', spli...  11.5 us
    all_to_all x1, waiting for transfers between devices, body(): lax.all_to_all(expert_out.reshape(experts, per_pair, feature_width), 'ep'...  7.62 us
    all_to_all x1, starting transfers between devices, body(): lax.all_to_all(token_part.reshape(experts, per_pair, feature_width), 'ep'...  4.41 us
    all_to_all x1, starting transfers between devices, body(): lax.all_to_all(expert_out.reshape(experts, per_pair, feature_width), 'ep'...  4.24 us
  transfers between devices with their start and end apart: 10, of which 4 were waited for; matrix products, arithmetic and copies ran while one was open for 40% of the time, Pallas kernels for 0%

commit v1 on v0

--- a/solution.py
+++ b/solution.py
@@ -4,6 +4,18 @@
 from jax.sharding import PartitionSpec as P
 
 STRIPE = 16
+
+
+def area_draw(z_in, on_dim, frame):
+    taken_in, r1 = (z_in.shape[:on_dim], z_in.shape[on_dim + 1 :])
+    frame_out = z_in.reshape(*taken_in, frame, -1, *r1)
+    return jnp.moveaxis(frame_out, on_dim, 0)
+
+
+def expand_chunk(mine_x, row_dim):
+    t1 = list(mine_x.shape[1:])
+    t1[row_dim] *= mine_x.shape[0]
+    return jnp.moveaxis(mine_x, 0, row_dim).reshape(t1)
 
 
 def silu_grad(value):
@@ -87,12 +99,23 @@
     hidden = (activated * pre_up).astype(jnp.bfloat16)
     expert_out = matmul(hidden, down_mat).astype(jnp.bfloat16)
     expert_out, grad_in = lax.optimization_barrier((expert_out, grad_in))
-    returned = lax.all_to_all(
-        expert_out.reshape(experts, per_pair, feature_width),
-        "ep",
-        split_axis=0,
-        concat_axis=0,
-        tiled=True,
+
+    def carry_the_frames(x_in, group_axis, inputs, chunk=0):
+        upper = lax.psum(1, group_axis)
+        block_next = lax.axis_index(group_axis)
+        w_next, tmp = (upper, block_next)
+        kept_arr = area_draw(x_in, inputs, w_next)
+        current_arr = kept_arr
+        for s in range(1, w_next):
+            finding, extra = ((tmp + s) % w_next, (tmp - s) % w_next)
+            all_values = lax.dynamic_index_in_dim(kept_arr, finding, 0)
+            mat_out = list(map(lambda jj: (jj, (jj + s) % w_next), range(w_next)))
+            d_next = lax.ppermute(all_values, group_axis, mat_out)
+            current_arr = lax.dynamic_update_slice_in_dim(current_arr, d_next, extra, axis=0)
+        return expand_chunk(current_arr, chunk)
+
+    returned = carry_the_frames(
+        expert_out.reshape(experts, per_pair, feature_width), "ep", 0
     ).reshape(total_slots, feature_width)
     hidden_grad = rows_times(grad_in, down_mat)
     gate_pre_grad = (hidden_grad * pre_up * silu_grad(pre_gate)).astype(jnp.bfloat16)

time: 130 us -> 170 us (1.31)
  waiting for transfers between devices: 45.1 us -> 79 us
  starting transfers between devices: 23.8 us -> 32.5 us
  matrix products: 49.9 us -> 46.1 us
    ppermute x0 -> x7, waiting for transfers between devices: none -> 44 us  [carry_the_frames(): d_next = lax.ppermute(all_values, group_axis, mat_out)]
    ppermute x0 -> x7, starting transfers between devices: none -> 12.6 us  [carry_the_frames(): d_next = lax.ppermute(all_values, group_axis, mat_out)]
    all_to_all x1 -> x0, waiting for transfers between devices: 7.62 us -> none  [body(): lax.all_to_all(expert_out.reshape(experts, per_pair, feature_width), 'ep'...]
    all_to_all x1 -> x0, starting transfers between devices: 4.24 us -> none  [body(): lax.all_to_all(expert_out.reshape(experts, per_pair, feature_width), 'ep'...]
    dot_general x8, matrix products: 15.1 us -> 12.2 us  [inner_rows(): lax.dot_general(left, right, (((0,), (0,)), ((), ())), preferred_element_...]
    all_to_all x1, waiting for transfers between devices: 2.11 us -> 0.01 us  [body(): lax.all_to_all(token_part.reshape(experts, per_pair, feature_width), 'ep'...]
  transfers between devices with their start and end apart: 10 -> 16, of which waited for: 4 -> 8; matrix products, arithmetic and copies ran while one was open for 40% -> 29% of each run, Pallas kernels for 0% -> 0%
where the time goes in v1:
time: 170 us
  waiting for transfers between devices  79 us (46%)
  matrix products  46.1 us (27%)
  starting transfers between devices  32.5 us (19%)
  local copies, waits for them, and re-layouts  8.69 us (5%)
  other arithmetic  1.95 us (1%)
    ppermute x7, waiting for transfers between devices, carry_the_frames(): d_next = lax.ppermute(all_values, group_axis, mat_out)  44 us
    all_to_all x2, waiting for transfers between devices, exchange(): lax.all_to_all(rows.reshape(experts, per_pair, feature_width), 'ep', spli...  35.1 us
    dot_general x10, matrix products, rows_times(): lax.dot_general(left, right, (((1,), (1,)), ((), ())), preferred_element_...  19.5 us
    dot_general x7, matrix products, matmul(): return jnp.dot(left, right, preferred_element_type=jnp.float32)  14.4 us
    ppermute x7, starting transfers between devices, carry_the_frames(): d_next = lax.ppermute(all_values, group_axis, mat_out)  12.6 us
    dot_general x8, matrix products, inner_rows(): lax.dot_general(left, right, (((0,), (0,)), ((), ())), preferred_element_...  12.2 us
    all_to_all x2, starting transfers between devices, exchange(): lax.all_to_all(rows.reshape(experts, per_pair, feature_width), 'ep', spli...  11.5 us
    all_to_all x1, starting transfers between devices, body(): lax.all_to_all(token_part.reshape(experts, per_pair, feature_width), 'ep'...  4.79 us
  transfers between devices with their start and end apart: 16, of which 8 were waited for; matrix products, arithmetic and copies ran while one was open for 29% of the time, Pallas kernels for 0%

profile of v1, /device:TPU:0, one launch (start us, length us, event | category | flops | bytes accessed | tf_op | source)
XLA Modules:
  0.0 169.6 jit_solution(6034154104342461595)
XLA Ops:
  1.7 2.6 %convolution_convert_fusion.1 = bf16[256,2048]{1,0:T(8,128)(2,1)} fusion(bf16[256,2048]{1,0:T(8,128)(2,1)} %param.7, s32[256]{0:T(256)S(1)} %compare_select_fusion.1), kind=kOutput, calls=%fused_computation.14 | convolution fusion | flops 269025280 | bytes 2098176 | tf_op jit(solution)/shard_map/dot_general | solution.py:39
  4.4 7.3 %all-to-all-start = ((bf16[8,32,2048]{2,1,0:T(8,128)(2,1)}), bf16[8,32,2048]{2,1,0:T(8,128)(2,1)}, u32[]{:S(2)}, u32[]{:S(2)}) async-start(bf16[8,32,2048]{2,1,0:T(8,128)(2,1)} %bitcast.75), calls=%async_computation | async-start | bytes 2097152 | tf_op jit(solution)/shard_map/all_to_all | solution.py:68
  12.4 2.6 %fusion.6 = bf16[256,2048]{1,0:T(8,128)(2,1)} fusion(bf16[256,2048]{1,0:T(8,128)(2,1)} %param.13, f32[256]{0:T(256)S(1)} %select_reduce_fusion, s32[256]{0:T(256)S(1)} %compare_select_fusion.1), kind=kOutput, calls=%fused_computation.11 | convolution fusion | flops 269549568 | bytes 2099200 | tf_op jit(solution)/shard_map/dot_general | solution.py:39
  15.1 22.4 %all-to-all-done = bf16[8,32,2048]{2,1,0:T(8,128)(2,1)} async-done(((bf16[8,32,2048]{2,1,0:T(8,128)(2,1)}), bf16[8,32,2048]{2,1,0:T(8,128)(2,1)}, u32[]{:S(2)}, u32[]{:S(2)}) %all-to-all-start) | async-done | bytes 1048608 | tf_op jit(solution)/shard_map/all_to_all | solution.py:68
  37.5 4.2 %all-to-all-start.1 = ((bf16[8,32,2048]{2,1,0:T(8,128)(2,1)}), bf16[8,32,2048]{2,1,0:T(8,128)(2,1)}, u32[]{:S(2)}, u32[]{:S(2)}) async-start(bf16[8,32,2048]{2,1,0:T(8,128)(2,1)} %bitcast.74), calls=%async_computation.1 | async-start | bytes 2097152 | tf_op jit(solution)/shard_map/all_to_all | solution.py:68
  43.1 2.8 %dynamic-slice_bitcast_fusion = (bf16[192,2048]{1,0:T(8,128)(2,1)}, bf16[192,2048]{1,0:T(8,128)(2,1)}) fusion(bf16[1,768,2048]{2,1,0:T(8,128)(2,1)} %param.11, s32[]{:T(128)S(6)} %select_n.158, bf16[1,768,2048]{2,1,0:T(8,128)(2,1)} %param.10), kind=kLoop, calls=%fused_computation.37 | loop fusion | bytes 3145732 | tf_op jit(solution)/shard_map/dynamic_slice | solution.py:166
  47.4 4.0 %fusion.1 = f32[256,1536]{1,0:T(8,128)S(1)} fusion(bf16[256,2048]{1,0:T(8,128)(2,1)} %bitcast.5, bf16[768,2048]{1,0:T(8,128)(2,1)S(1)} %bitcast.80, bf16[768,2048]{1,0:T(8,128)(2,1)} %bitcast.82), kind=kOutput, calls=%fused_computation.2 | convolution fusion | flops 1623195648 | bytes 8912896 | tf_op jit(solution)/shard_map/dot_general | solution.py:27
  52.7 2.0 %fusion.9 = bf16[256,2048]{1,0:T(8,128)(2,1)} fusion(bf16[1,768,2048]{2,1,0:T(8,128)(2,1)S(1)} %copy-done, f32[256,1536]{1,0:T(8,128)S(1)} %fusion.1), kind=kOutput, calls=%fused_computation.16 | convolution fusion | flops 807010304 | bytes 5767168 | tf_op jit(solution)/shard_map/dot_general | solution.py:39
  54.7 12.6 %all-to-all-done.1 = bf16[8,32,2048]{2,1,0:T(8,128)(2,1)} async-done(((bf16[8,32,2048]{2,1,0:T(8,128)(2,1)}), bf16[8,32,2048]{2,1,0:T(8,128)(2,1)}, u32[]{:S(2)}, u32[]{:S(2)}) %all-to-all-start.1) | async-done | bytes 1048608 | tf_op jit(solution)/shard_map/all_to_all | solution.py:68
  67.3 3.0 %multiply_convert_fusion.1 = (bf16[256,768]{1,0:T(8,128)(2,1)S(1)}, bf16[256,768]{1,0:T(8,128)(2,1)S(1)}) fusion(f32[256,1536]{1,0:T(8,128)} %copy-done.8, bf16[256,2048]{1,0:T(8,128)(2,1)} %bitcast.10, bf16[1,768,2048]{2,1,0:T(8,128)(2,1)S(1)} %copy-done), kind=kOutput, calls=%fused_computation.40 | convolution fusion | flops 807862272 | bytes 6553600 | tf_op jit(solution)/shard_map/dot_general | solution.py:27
  71.0 2.8 %fusion.7 = bf16[256,2048]{1,0:T(8,128)(2,1)} fusion(bf16[768,2048]{1,0:T(8,128)(2,1)S(1)} %bitcast.81, bf16[768,2048]{1,0:T(8,128)(2,1)S(1)} %bitcast.83, bf16[256,768]{1,0:T(8,128)(2,1)S(1)} %get-tuple-element.35, bf16[256,768]{1,0:T(8,128)(2,1)S(1)} %get-tuple-element.34), kind=kOutput, calls=%fused_computation.12 | convolution fusion | flops 1625292800 | bytes 8126464 | tf_op jit(solution)/shard_map/dot_general | solution.py:39
  77.5 4.8 %all-to-all-start.2 = ((bf16[8,32,2048]{2,1,0:T(8,128)(2,1)}), bf16[8,32,2048]{2,1,0:T(8,128)(2,1)}, u32[]{:S(2)}, u32[]{:S(2)}) async-start(bf16[8,32,2048]{2,1,0:T(8,128)(2,1)} %bitcast.79), calls=%async_computation.2 | async-start | bytes 2097152 | tf_op jit(solution)/shard_map/all_to_all | solution.py:130
  82.2 2.3 %fusion.84 = f32[256,384]{0,1:T(8,128)S(1)} fusion(bf16[256,2048]{1,0:T(8,128)(2,1)} %bitcast.5, bf16[192,2048]{1,0:T(8,128)(2,1)} %get-tuple-element.55, bf16[192,2048]{1,0:T(8,128)(2,1)} %get-tuple-element.56), kind=kOutput, calls=%fused_computation.132 | convolution fusion | flops 405798912 | bytes 3014656 | tf_op jit(solution)/shard_map/dot_general | solution.py:27
  84.6 1.8 %multiply_convert_fusion.15 = (bf16[256,192]{0,1:T(8,128)(2,1)S(1)}, bf16[256,192]{0,1:T(8,128)(2,1)S(1)}) fusion(f32[256,384]{0,1:T(8,128)S(1)} %fusion.84, bf16[256,2048]{1,0:T(8,128)(2,1)} %bitcast.10, bf16[1,768,2048]{2,1,0:T(8,128)(2,1)S(1)} %copy-done, s32[]{:T(128)S(6)} %select_n.158), kind=kOutput, calls=%fused_computation.86 | convolution fusion | flops 201965568 | bytes 2424836 | tf_op jit(solution)/shard_map/dot_general | solution.py:27
  86.4 1.8 %fusion.32 = f32[384,2048]{1,0:T(8,128)S(1)} fusion(bf16[256,2048]{1,0:T(8,128)(2,1)} %bitcast.5, bf16[256,192]{0,1:T(8,128)(2,1)S(1)} %get-tuple-element.50, bf16[256,192]{0,1:T(8,128)(2,1)S(1)} %get-tuple-element.49), kind=kOutput, calls=%fused_computation.53 | convolution fusion | flops 403046400 | bytes 4390912 | tf_op jit(solution)/shard_map/dot_general | solution.py:33
  88.3 2.1 %collective-permute-start.1 = (bf16[1,1,32,2048]{3,2,0,1:T(8,128)(2,1)S(1)}, bf16[1,1,32,2048]{3,2,0,1:T(8,128)(2,1)S(1)}, u32[]{:S(2)}, u32[]{:S(2)}) collective-permute-start(bf16[1,1,32,2048]{3,2,0,1:T(8,128)(2,1)S(1)} %get-tuple-element.43), channel_id=1, source_target_pairs={{0,2},{1,3},{2,4},{3,5},{4,6},{5,7},{6,0},{7,1},{8,10},{9,11},{10,... | collective-permute-start | bytes 393224 | tf_op jit(solution)/shard_map/ppermute | solution.py:113
  92.0 14.6 %collective-permute-done.1 = bf16[1,1,32,2048]{3,2,0,1:T(8,128)(2,1)S(1)} collective-permute-done((bf16[1,1,32,2048]{3,2,0,1:T(8,128)(2,1)S(1)}, bf16[1,1,32,2048]{3,2,0,1:T(8,128)(2,1)S(1)}, u32[]{:S(2)}, u32[]{:S(2)}) %collective-permute-start.1) | collective-permute-done | bytes 131104 | tf_op jit(solution)/shard_map/ppermute | solution.py:113
  106.6 4.1 %collective-permute-start.2 = (bf16[1,1,32,2048]{3,2,0,1:T(8,128)(2,1)S(1)}, bf16[1,1,32,2048]{3,2,0,1:T(8,128)(2,1)S(1)}, u32[]{:S(2)}, u32[]{:S(2)}) collective-permute-start(bf16[1,1,32,2048]{3,2,0,1:T(8,128)(2,1)S(1)} %get-tuple-element.42), channel_id=1, source_target_pairs={{0,3},{1,4},{2,5},{3,6},{4,7},{5,0},{6,1},{7,2},{8,11},{9,12},{10,... | collective-permute-start | bytes 393224 | tf_op jit(solution)/shard_map/ppermute | solution.py:113
  110.8 8.4 %collective-permute-done.2 = bf16[1,1,32,2048]{3,2,0,1:T(8,128)(2,1)S(1)} collective-permute-done((bf16[1,1,32,2048]{3,2,0,1:T(8,128)(2,1)S(1)}, bf16[1,1,32,2048]{3,2,0,1:T(8,128)(2,1)S(1)}, u32[]{:S(2)}, u32[]{:S(2)}) %collective-permute-start.2) | collective-permute-done | bytes 131104 | tf_op jit(solution)/shard_map/ppermute | solution.py:113
  119.3 7.7 %collective-permute-done.3 = bf16[1,1,32,2048]{3,2,0,1:T(8,128)(2,1)S(1)} collective-permute-done((bf16[1,1,32,2048]{3,2,0,1:T(8,128)(2,1)S(1)}, bf16[1,1,32,2048]{3,2,0,1:T(8,128)(2,1)S(1)}, u32[]{:S(2)}, u32[]{:S(2)}) %collective-permute-start.3) | collective-permute-done | bytes 131104 | tf_op jit(solution)/shard_map/ppermute | solution.py:113
  127.0 5.8 %collective-permute-done.4 = bf16[1,1,32,2048]{3,2,0,1:T(8,128)(2,1)S(1)} collective-permute-done((bf16[1,1,32,2048]{3,2,0,1:T(8,128)(2,1)S(1)}, bf16[1,1,32,2048]{3,2,0,1:T(8,128)(2,1)S(1)}, u32[]{:S(2)}, u32[]{:S(2)}) %collective-permute-start.4) | collective-permute-done | bytes 131104 | tf_op jit(solution)/shard_map/ppermute | solution.py:113
  132.9 4.9 %collective-permute-done.5 = bf16[1,1,32,2048]{3,2,0,1:T(8,128)(2,1)S(1)} collective-permute-done((bf16[1,1,32,2048]{3,2,0,1:T(8,128)(2,1)S(1)}, bf16[1,1,32,2048]{3,2,0,1:T(8,128)(2,1)S(1)}, u32[]{:S(2)}, u32[]{:S(2)}) %collective-permute-start.5) | collective-permute-done | bytes 131104 | tf_op jit(solution)/shard_map/ppermute | solution.py:113
  137.8 5.0 %collective-permute-start.6 = (bf16[1,1,32,2048]{3,2,0,1:T(8,128)(2,1)S(1)}, bf16[1,1,32,2048]{3,2,0,1:T(8,128)(2,1)S(1)}, u32[]{:S(2)}, u32[]{:S(2)}) collective-permute-start(bf16[1,1,32,2048]{3,2,0,1:T(8,128)(2,1)S(1)} %get-tuple-element.38), channel_id=1, source_target_pairs={{0,7},{1,0},{2,1},{3,2},{4,3},{5,4},{6,5},{7,6},{8,15},{9,8},{10,9... | collective-permute-start | bytes 393224 | tf_op jit(solution)/shard_map/ppermute | solution.py:113
  142.8 2.5 %collective-permute-done.6 = bf16[1,1,32,2048]{3,2,0,1:T(8,128)(2,1)S(1)} collective-permute-done((bf16[1,1,32,2048]{3,2,0,1:T(8,128)(2,1)S(1)}, bf16[1,1,32,2048]{3,2,0,1:T(8,128)(2,1)S(1)}, u32[]{:S(2)}, u32[]{:S(2)}) %collective-permute-start.6) | collective-permute-done | bytes 131104 | tf_op jit(solution)/shard_map/ppermute | solution.py:113
  146.8 1.8 %fusion.82 = f32[256,384]{0,1:T(8,128)S(1)} fusion(bf16[256,2048]{1,0:T(8,128)(2,1)} %collective-permute-done.9, bf16[192,2048]{1,0:T(8,128)(2,1)S(1)} %copy-done.3, bf16[192,2048]{1,0:T(8,128)(2,1)S(1)} %copy-done.4), kind=kOutput, calls=%fused_computation.130 | convolution fusion | flops 405798912 | bytes 3014656 | tf_op jit(solution)/shard_map/dot_general | solution.py:27
  148.8 1.8 %fusion.83 = f32[256,384]{0,1:T(8,128)S(1)} fusion(bf16[256,2048]{1,0:T(8,128)(2,1)} %collective-permute-done.7, bf16[192,2048]{1,0:T(8,128)(2,1)S(1)} %copy-done.3, bf16[192,2048]{1,0:T(8,128)(2,1)S(1)} %copy-done.4), kind=kOutput, calls=%fused_computation.131 | convolution fusion | flops 405798912 | bytes 3014656 | tf_op jit(solution)/shard_map/dot_general | solution.py:27
  151.2 1.7 %multiply_convert_fusion.11 = (bf16[256,192]{0,1:T(8,128)(2,1)S(1)}, bf16[256,192]{0,1:T(8,128)(2,1)S(1)}) fusion(f32[256,384]{0,1:T(8,128)S(1)} %fusion.82, bf16[256,2048]{1,0:T(8,128)(2,1)} %collective-permute-done.10, bf16[1,768,2048]{2,1,0:T(8,128)(2,1)S(1)} %copy-done, s32[]{:T(128)S(6)} %select_n.158), kind=kOutput, calls=%fused_computation.78 | convolution fusion | flops 201965568 | bytes 2424836 | tf_op jit(solution)/shard_map/dot_general | solution.py:27
  152.9 1.8 %multiply_convert_fusion.13 = (bf16[256,192]{0,1:T(8,128)(2,1)S(1)}, bf16[256,192]{0,1:T(8,128)(2,1)S(1)}) fusion(f32[256,384]{0,1:T(8,128)S(1)} %fusion.83, bf16[256,2048]{1,0:T(8,128)(2,1)} %collective-permute-done.8, bf16[1,768,2048]{2,1,0:T(8,128)(2,1)S(1)} %copy-done, s32[]{:T(128)S(6)} %select_n.158), kind=kOutput, calls=%fused_computation.82 | convolution fusion | flops 201965568 | bytes 2424836 | tf_op jit(solution)/shard_map/dot_general | solution.py:27
  154.7 1.8 %fusion.36 = f32[384,2048]{1,0:T(8,128)S(1)} fusion(bf16[256,2048]{1,0:T(8,128)(2,1)} %collective-permute-done.7, bf16[256,192]{0,1:T(8,128)(2,1)S(1)} %get-tuple-element.48, bf16[256,192]{0,1:T(8,128)(2,1)S(1)} %get-tuple-element.47), kind=kOutput, calls=%fused_computation.57 | convolution fusion | flops 403046400 | bytes 4390912 | tf_op jit(solution)/shard_map/dot_general | solution.py:33
  157.5 1.8 %fusion.40 = f32[384,2048]{1,0:T(8,128)S(1)} fusion(bf16[256,2048]{1,0:T(8,128)(2,1)} %collective-permute-done.9, bf16[256,192]{0,1:T(8,128)(2,1)S(1)} %get-tuple-element.52, bf16[256,192]{0,1:T(8,128)(2,1)S(1)} %get-tuple-element.51), kind=kOutput, calls=%fused_computation.61 | convolution fusion | flops 403046400 | bytes 4390912 | tf_op jit(solution)/shard_map/dot_general | solution.py:33
  162.5 2.5 %fusion.13 = bf16[1,192,2048]{2,1,0:T(8,128)(2,1)} fusion(f32[192,2048]{1,0:T(8,128)S(1)} %fusion.59, f32[192,2048]{1,0:T(8,128)S(1)} %convolution_add_fusion.1, bf16[256,2048]{1,0:T(8,128)(2,1)} %collective-permute-done.10, f32[256,384]{0,1:T(8,128)S(1)} %fusion.82), kind=kOutput, calls=%fused_computation.18 | convolution fusion | flops 202801152 | bytes 5373952 | tf_op jit(solution)/shard_map/dot_general | solution.py:33
  166.9 2.7 %convolution_convert_fusion = bf16[256,2048]{1,0:T(8,128)(2,1)} fusion(bf16[256,2048]{1,0:T(8,128)(2,1)} %bitcast.14, s32[256]{0:T(256)S(1)} %bitcast.85), kind=kOutput, calls=%fused_computation.13 | convolution fusion | flops 269025280 | bytes 2098176 | tf_op jit(solution)/shard_map/dot_general | solution.py:39
  (66 shorter events, 20.0 us)
Async XLA Ops:
  0.6 52.0 %copy-start = (bf16[1,768,2048]{2,1,0:T(8,128)(2,1)S(1)}, bf16[1,768,2048]{2,1,0:T(8,128)(2,1)}, u32[]{:S(2)}) copy-start(bf16[1,768,2048]{2,1,0:T(8,128)(2,1)} %param.12) | copy-start | bytes 9437188
  4.4 33.1 %all-to-all-start = ((bf16[8,32,2048]{2,1,0:T(8,128)(2,1)}), bf16[8,32,2048]{2,1,0:T(8,128)(2,1)}, u32[]{:S(2)}, u32[]{:S(2)}) async-start(bf16[8,32,2048]{2,1,0:T(8,128)(2,1)} %bitcast.75), calls=%async_computation | async-start | bytes 2097152 | tf_op jit(solution)/shard_map/all_to_all | solution.py:68
  37.5 29.9 %all-to-all-start.1 = ((bf16[8,32,2048]{2,1,0:T(8,128)(2,1)}), bf16[8,32,2048]{2,1,0:T(8,128)(2,1)}, u32[]{:S(2)}, u32[]{:S(2)}) async-start(bf16[8,32,2048]{2,1,0:T(8,128)(2,1)} %bitcast.74), calls=%async_computation.1 | async-start | bytes 2097152 | tf_op jit(solution)/shard_map/all_to_all | solution.py:68
  42.3 5.2 %copy-start.5 = (bf16[1,768,2048]{2,1,0:T(8,128)(2,1)S(1)}, bf16[1,768,2048]{2,1,0:T(8,128)(2,1)}, u32[]{:S(2)}) copy-start(bf16[1,768,2048]{2,1,0:T(8,128)(2,1)} %param.11) | copy-start | bytes 9437188
  45.9 100.9 %collective-permute-start.9 = (bf16[256,2048]{1,0:T(8,128)(2,1)}, bf16[256,2048]{1,0:T(8,128)(2,1)}, u32[]{:S(2)}, u32[]{:S(2)}) collective-permute-start(bf16[256,2048]{1,0:T(8,128)(2,1)} %bitcast.5), channel_id=1, source_target_pairs={{0,16},{8,24},{16,0},{24,8},{1,17},{9,25},{17,1},{25,9},{2,18},{10... | collective-permute-start | bytes 3145736 | tf_op jit(solution)/shard_map/ppermute | solution.py:82
  47.4 97.9 %collective-permute-start.7 = (bf16[256,2048]{1,0:T(8,128)(2,1)}, bf16[256,2048]{1,0:T(8,128)(2,1)}, u32[]{:S(2)}, u32[]{:S(2)}) collective-permute-start(bf16[256,2048]{1,0:T(8,128)(2,1)} %bitcast.5), channel_id=1, source_target_pairs={{0,8},{8,0},{16,24},{24,16},{1,9},{9,1},{17,25},{25,17},{2,10},{10... | collective-permute-start | bytes 3145736 | tf_op jit(solution)/shard_map/ppermute | solution.py:82
  51.5 1.2 copy-start.8
  67.3 3.0 %copy-start.6 = (bf16[1,768,2048]{2,1,0:T(8,128)(2,1)S(1)}, bf16[1,768,2048]{2,1,0:T(8,128)(2,1)}, u32[]{:S(2)}) copy-start(bf16[1,768,2048]{2,1,0:T(8,128)(2,1)} %param.11) | copy-start | bytes 9437188
  67.3 3.6 %copy-start.7 = (bf16[1,768,2048]{2,1,0:T(8,128)(2,1)S(1)}, bf16[1,768,2048]{2,1,0:T(8,128)(2,1)}, u32[]{:S(2)}) copy-start(bf16[1,768,2048]{2,1,0:T(8,128)(2,1)} %param.10) | copy-start | bytes 9437188
  73.8 73.1 %collective-permute-start.10 = (bf16[256,2048]{1,0:T(8,128)(2,1)}, bf16[256,2048]{1,0:T(8,128)(2,1)}, u32[]{:S(2)}, u32[]{:S(2)}) collective-permute-start(bf16[256,2048]{1,0:T(8,128)(2,1)} %bitcast.10), channel_id=1, source_target_pairs={{0,16},{8,24},{16,0},{24,8},{1,17},{9,25},{17,1},{25,9},{2,18},{10... | collective-permute-start | bytes 3145736 | tf_op jit(solution)/shard_map/ppermute | solution.py:82
  75.3 70.1 %collective-permute-start.8 = (bf16[256,2048]{1,0:T(8,128)(2,1)}, bf16[256,2048]{1,0:T(8,128)(2,1)}, u32[]{:S(2)}, u32[]{:S(2)}) collective-permute-start(bf16[256,2048]{1,0:T(8,128)(2,1)} %bitcast.10), channel_id=1, source_target_pairs={{0,8},{8,0},{16,24},{24,16},{1,9},{9,1},{17,25},{25,17},{2,10},{10... | collective-permute-start | bytes 3145736 | tf_op jit(solution)/shard_map/ppermute | solution.py:82
  76.2 12.0 %collective-permute-start = (bf16[1,1,32,2048]{3,2,0,1:T(8,128)(2,1)S(1)}, bf16[1,1,32,2048]{3,2,0,1:T(8,128)(2,1)S(1)}, u32[]{:S(2)}, u32[]{:S(2)}) collective-permute-start(bf16[1,1,32,2048]{3,2,0,1:T(8,128)(2,1)S(1)} %constant_dynamic-slice_fusion.6), channel_id=1, source_target_pairs={{0,1},{1,2},{2,3},{3,4},{4,5},{5,6},{6,7},{7,0},{8,9},{9,10},{10,1... | collective-permute-start | bytes 393224 | tf_op jit(solution)/shard_map/ppermute | solution.py:113
  77.5 89.5 %all-to-all-start.2 = ((bf16[8,32,2048]{2,1,0:T(8,128)(2,1)}), bf16[8,32,2048]{2,1,0:T(8,128)(2,1)}, u32[]{:S(2)}, u32[]{:S(2)}) async-start(bf16[8,32,2048]{2,1,0:T(8,128)(2,1)} %bitcast.79), calls=%async_computation.2 | async-start | bytes 2097152 | tf_op jit(solution)/shard_map/all_to_all | solution.py:130
  84.5 3.7 %copy-start.2 = (bf16[256,2048]{1,0:T(8,128)(2,1)S(1)}, bf16[256,2048]{1,0:T(8,128)(2,1)}, u32[]{:S(2)}) copy-start(bf16[256,2048]{1,0:T(8,128)(2,1)} %fusion.9) | copy-start | bytes 3145732
  88.3 18.3 %collective-permute-start.1 = (bf16[1,1,32,2048]{3,2,0,1:T(8,128)(2,1)S(1)}, bf16[1,1,32,2048]{3,2,0,1:T(8,128)(2,1)S(1)}, u32[]{:S(2)}, u32[]{:S(2)}) collective-permute-start(bf16[1,1,32,2048]{3,2,0,1:T(8,128)(2,1)S(1)} %get-tuple-element.43), channel_id=1, source_target_pairs={{0,2},{1,3},{2,4},{3,5},{4,6},{5,7},{6,0},{7,1},{8,10},{9,11},{10,... | collective-permute-start | bytes 393224 | tf_op jit(solution)/shard_map/ppermute | solution.py:113
  92.0 54.8 %copy-start.3 = (bf16[192,2048]{1,0:T(8,128)(2,1)S(1)}, bf16[192,2048]{1,0:T(8,128)(2,1)}, u32[]{:S(2)}) copy-start(bf16[192,2048]{1,0:T(8,128)(2,1)} %get-tuple-element.55) | copy-start | bytes 2359300
  92.0 54.8 %copy-start.4 = (bf16[192,2048]{1,0:T(8,128)(2,1)S(1)}, bf16[192,2048]{1,0:T(8,128)(2,1)}, u32[]{:S(2)}) copy-start(bf16[192,2048]{1,0:T(8,128)(2,1)} %get-tuple-element.56) | copy-start | bytes 2359300
  106.6 12.5 %collective-permute-start.2 = (bf16[1,1,32,2048]{3,2,0,1:T(8,128)(2,1)S(1)}, bf16[1,1,32,2048]{3,2,0,1:T(8,128)(2,1)S(1)}, u32[]{:S(2)}, u32[]{:S(2)}) collective-permute-start(bf16[1,1,32,2048]{3,2,0,1:T(8,128)(2,1)S(1)} %get-tuple-element.42), channel_id=1, source_target_pairs={{0,3},{1,4},{2,5},{3,6},{4,7},{5,0},{6,1},{7,2},{8,11},{9,12},{10,... | collective-permute-start | bytes 393224 | tf_op jit(solution)/shard_map/ppermute | solution.py:113
  119.2 7.8 %collective-permute-start.3 = (bf16[1,1,32,2048]{3,2,0,1:T(8,128)(2,1)S(1)}, bf16[1,1,32,2048]{3,2,0,1:T(8,128)(2,1)S(1)}, u32[]{:S(2)}, u32[]{:S(2)}) collective-permute-start(bf16[1,1,32,2048]{3,2,0,1:T(8,128)(2,1)S(1)} %get-tuple-element.41), channel_id=1, source_target_pairs={{0,4},{1,5},{2,6},{3,7},{4,0},{5,1},{6,2},{7,3},{8,12},{9,13},{10,... | collective-permute-start | bytes 393224 | tf_op jit(solution)/shard_map/ppermute | solution.py:113
  127.0 5.9 %collective-permute-start.4 = (bf16[1,1,32,2048]{3,2,0,1:T(8,128)(2,1)S(1)}, bf16[1,1,32,2048]{3,2,0,1:T(8,128)(2,1)S(1)}, u32[]{:S(2)}, u32[]{:S(2)}) collective-permute-start(bf16[1,1,32,2048]{3,2,0,1:T(8,128)(2,1)S(1)} %get-tuple-element.40), channel_id=1, source_target_pairs={{0,5},{1,6},{2,7},{3,0},{4,1},{5,2},{6,3},{7,4},{8,13},{9,14},{10,... | collective-permute-start | bytes 393224 | tf_op jit(solution)/shard_map/ppermute | solution.py:113
  132.9 5.0 %collective-permute-start.5 = (bf16[1,1,32,2048]{3,2,0,1:T(8,128)(2,1)S(1)}, bf16[1,1,32,2048]{3,2,0,1:T(8,128)(2,1)S(1)}, u32[]{:S(2)}, u32[]{:S(2)}) collective-permute-start(bf16[1,1,32,2048]{3,2,0,1:T(8,128)(2,1)S(1)} %get-tuple-element.39), channel_id=1, source_target_pairs={{0,6},{1,7},{2,0},{3,1},{4,2},{5,3},{6,4},{7,5},{8,14},{9,15},{10,... | collective-permute-start | bytes 393224 | tf_op jit(solution)/shard_map/ppermute | solution.py:113
  137.8 7.5 %collective-permute-start.6 = (bf16[1,1,32,2048]{3,2,0,1:T(8,128)(2,1)S(1)}, bf16[1,1,32,2048]{3,2,0,1:T(8,128)(2,1)S(1)}, u32[]{:S(2)}, u32[]{:S(2)}) collective-permute-start(bf16[1,1,32,2048]{3,2,0,1:T(8,128)(2,1)S(1)} %get-tuple-element.38), channel_id=1, source_target_pairs={{0,7},{1,0},{2,1},{3,2},{4,3},{5,4},{6,5},{7,6},{8,15},{9,8},{10,9... | collective-permute-start | bytes 393224 | tf_op jit(solution)/shard_map/ppermute | solution.py:113
  148.7 12.3 %collective-permute-start.12 = (bf16[256,2048]{1,0:T(8,128)(2,1)}, bf16[256,2048]{1,0:T(8,128)(2,1)S(1)}, u32[]{:S(2)}, u32[]{:S(2)}) collective-permute-start(bf16[256,2048]{1,0:T(8,128)(2,1)} %collective-permute-done.9), channel_id=1, source_target_pairs={{0,8},{8,0},{16,24},{24,16},{1,9},{9,1},{17,25},{25,17},{2,10},{10... | collective-permute-start | bytes 3145736 | tf_op jit(solution)/shard_map/ppermute | solution.py:82
  150.6 11.0 %collective-permute-start.11 = (bf16[256,2048]{1,0:T(8,128)(2,1)}, bf16[256,2048]{1,0:T(8,128)(2,1)S(1)}, u32[]{:S(2)}, u32[]{:S(2)}) collective-permute-start(bf16[256,2048]{1,0:T(8,128)(2,1)} %collective-permute-done.10), channel_id=1, source_target_pairs={{0,8},{8,0},{16,24},{24,16},{1,9},{9,1},{17,25},{25,17},{2,10},{10... | collective-permute-start | bytes 3145736 | tf_op jit(solution)/shard_map/ppermute | solution.py:82
  152.9 3.6 %copy-start.1 = (bf16[256,2048]{1,0:T(8,128)(2,1)S(1)}, bf16[256,2048]{1,0:T(8,128)(2,1)}, u32[]{:S(2)}) copy-start(bf16[256,2048]{1,0:T(8,128)(2,1)} %param.13) | copy-start | bytes 3145732
